TPU v7x, 32 devices: a whole 2x2x4 slice. The times are simulated.
32 devices in a mesh: dp: 8 (over z, core), tensor: 4 (over y, x).
Axes of the slice: x: 2, y: 2, z: 4, core: 2. Of those that a mesh axis runs over, the one named last changes fastest.
Arguments:
- tokens: bfloat16 [512, 8192], P(None, 'dp'), may hold values from -6 to 6
- w_gate_up: bfloat16 [8192, 2, 28672], P('dp', None, 'tensor'), may hold values from -0.0625 to 0.0625
- w_down: bfloat16 [28672, 8192], P('tensor', 'dp'), may hold values from -0.03125 to 0.03125
- targets: bfloat16 [512, 8192], P(None, 'dp'), may hold values from -3 to 3
- proj_model: bfloat16 [8192, 128], P('dp'), may hold values from -0.0625 to 0.0625
- proj_hidden: bfloat16 [28672, 192], P('tensor'), may hold values from -0.03125 to 0.03125
- store: bfloat16 [4096, 12288], P(('dp', 'tensor')), may hold values from -0.017944336 to 0.017944336
Outputs:
- scores: float32 [4, 4096], P(None, ('dp', 'tensor'))
All inputs are finite; a program needn't handle non-finite values.
Results may differ from a plain program's by a relative error of at most 0.02.
Values may be sent and summed in bfloat16 or wider, within the bound.
No kernel may reach another device: no remote copies, remote signals or barrier semaphores. Data moves between devices by JAX's collectives and lax.ppermute only.
A program may use at most 256 MiB of HBM per device.

v0:
```python
import jax
import jax.numpy as jnp
import numpy as np
from jax import lax
from jax.sharding import Mesh, PartitionSpec as P

RANK = 64
SEQ = 128


def local(tokens, w_gate_up, w_down, targets, proj_model, proj_hidden, store):
    n_z = lax.axis_size("z")
    n_core = lax.axis_size("core")
    n_t = lax.axis_size("tensor")
    z = lax.axis_index("z")
    core = lax.axis_index("core")
    t_idx = lax.axis_index("tensor")
    total = tokens.shape[0]
    rows_z = total // n_z
    rows_t = total // n_t
    width_ff = w_down.shape[0]
    width_h = width_ff // n_core
    hi = lax.Precision.HIGHEST
    tests = total // SEQ

    def over_dp(part):
        part = lax.psum_scatter(
            part.reshape(total, n_core, width_h), "core", scatter_dimension=1, tiled=False
        )
        part = lax.psum_scatter(part.astype(jnp.bfloat16), "z", scatter_dimension=0, tiled=True)
        return part.astype(jnp.float32)

    a_in_part = jnp.dot(tokens, proj_model[:, :RANK], preferred_element_type=jnp.float32)
    gate = over_dp(jnp.dot(tokens, w_gate_up[:, 0, :], preferred_element_type=jnp.float32))
    up = over_dp(jnp.dot(tokens, w_gate_up[:, 1, :], preferred_element_type=jnp.float32))
    sig = jax.nn.sigmoid(gate)
    act = gate * sig
    hidden_loc = (act * up).astype(jnp.bfloat16)
    hidden = lax.all_gather(hidden_loc, "z", axis=0, tiled=True)
    hidden = lax.all_gather(hidden, "core", axis=1, tiled=True)
    out_part = jnp.dot(hidden, w_down, preferred_element_type=jnp.float32)
    out_rows = lax.psum_scatter(out_part, "tensor", scatter_dimension=0, tiled=True)
    tgt_rows = lax.dynamic_slice_in_dim(targets, t_idx * rows_t, rows_t, 0)
    cot_rows = (out_rows - tgt_rows.astype(jnp.float32)).astype(jnp.bfloat16)
    cot = lax.all_gather(cot_rows, "tensor", axis=0, tiled=True)
    a_out_part = jnp.dot(cot, proj_model[:, RANK:], preferred_element_type=jnp.float32)
    side = lax.psum(jnp.concatenate([a_in_part, a_out_part], axis=1), ("z", "core"))
    dh = over_dp(
        lax.dot_general(cot, w_down, (((1,), (1,)), ((), ())), preferred_element_type=jnp.float32)
    )
    dgate = (dh * up * sig * (1.0 + gate * (1.0 - sig))).astype(jnp.bfloat16)
    dup = (dh * act).astype(jnp.bfloat16)
    ph = lax.dynamic_slice_in_dim(proj_hidden, core * width_h, width_h, 0)
    b_part = jnp.concatenate(
        [
            jnp.dot(dgate, ph[:, :RANK], preferred_element_type=jnp.float32),
            jnp.dot(dup, ph[:, RANK : 2 * RANK], preferred_element_type=jnp.float32),
            jnp.dot(hidden_loc, ph[:, 2 * RANK :], preferred_element_type=jnp.float32),
        ],
        axis=1,
    )
    b_sum = lax.psum(b_part, ("core", "tensor"))
    side_z = lax.dynamic_slice_in_dim(side, z * rows_z, rows_z, 0)
    a_in = side_z[:, :RANK]
    a_out = side_z[:, RANK:]
    position = z * rows_z + lax.iota(jnp.int32, rows_z)
    member = ((position // SEQ)[:, None] == lax.iota(jnp.int32, tests)[None, :]).astype(jnp.float32)
    g_gate = jnp.einsum("ts,ti,tj->sij", member, a_in, b_sum[:, :RANK], precision=hi)
    g_up = jnp.einsum("ts,ti,tj->sij", member, a_in, b_sum[:, RANK : 2 * RANK], precision=hi)
    g_down = jnp.einsum("ts,ti,tj->sij", member, b_sum[:, 2 * RANK :], a_out, precision=hi)
    grads = lax.psum(jnp.stack([g_gate, g_up, g_down], axis=1).reshape(tests, 3 * RANK * RANK), "z")
    return lax.dot_general(
        grads.astype(jnp.bfloat16),
        store,
        (((1,), (1,)), ((), ())),
        preferred_element_type=jnp.float32,
    )


def solution(mesh):
    n_dp = mesh.shape["dp"]
    n_t = mesh.shape["tensor"]
    devices = np.asarray(mesh.devices).reshape(n_dp // 2, 2, n_t)
    fine = Mesh(devices, ("z", "core", "tensor"))
    dp = ("z", "core")
    return jax.shard_map(
        local,
        mesh=fine,
        in_specs=(
            P(None, dp),
            P(dp, None, "tensor"),
            P("tensor", dp),
            P(None, dp),
            P(dp, None),
            P("tensor", None),
            P(dp + ("tensor",), None),
        ),
        out_specs=P(None, dp + ("tensor",)),
        check_vma=False,
    )
```

profile of v0, /device:TPU:0, one launch (start us, length us, event | category | flops | bytes accessed | tf_op | source)
XLA Modules:
  0.0 831.2 jit_solution(7446013001953596638)
XLA Ops:
  6.5 55.9 %fusion.40 = (bf16[1024,1,7168]{2,1,0:T(2,128)(2,1)}, bf16[1024,1,7168]{2,1,0:T(2,128)(2,1)}) fusion(bf16[1024,2,7168]{2,1,0:T(2,128)(2,1)} %param.8), kind=kLoop, calls=%fused_computation.63 | loop fusion | bytes 58720256 | tf_op jit(solution)/shard_map/slice | solution.py:34
  62.4 60.0 %copy.21 = bf16[1024,1,7168]{0,2,1:T(8,128)(2,1)} copy(bf16[1024,1,7168]{2,1,0:T(2,128)(2,1)} %get-tuple-element.6) | data formatting | bytes 29360128 | tf_op jit(solution)/shard_map/dot_general | solution.py:35
  122.4 14.3 %fusion.9 = f32[512,2,3584]{2,0,1:T(8,128)} fusion(bf16[2,3584,1024]{2,1,0:T(8,128)(2,1)} %bitcast.58, bf16[512,1024]{1,0:T(8,128)(2,1)} %param.7), kind=kOutput, calls=%fused_computation.21 | convolution fusion | flops 7516192768 | bytes 30408704 | tf_op jit(solution)/shard_map/dot_general | solution.py:35
  136.8 61.2 %copy.20 = bf16[1024,1,7168]{0,2,1:T(8,128)(2,1)} copy(bf16[1024,1,7168]{2,1,0:T(2,128)(2,1)} %get-tuple-element.5) | data formatting | bytes 29360128 | tf_op jit(solution)/shard_map/dot_general | solution.py:34
  198.0 14.4 %fusion.11 = f32[512,2,3584]{2,0,1:T(8,128)} fusion(bf16[2,3584,1024]{2,1,0:T(8,128)(2,1)} %bitcast.59, bf16[512,1024]{1,0:T(8,128)(2,1)} %param.7), kind=kOutput, calls=%fused_computation.23 | convolution fusion | flops 7516192768 | bytes 30408704 | tf_op jit(solution)/shard_map/dot_general | solution.py:34
  212.4 5.4 convert_bitcast_fusion.1
  217.9 21.3 %reduce-scatter.8.cloned.1.call-done = f32[512,1,3584]{2,0,1:T(8,128)} async-done(((f32[512,2,3584]{2,0,1:T(8,128)}), f32[512,1,3584]{2,0,1:T(8,128)}) %reduce-scatter.8.cloned.1.call-update) | async-done | bytes 7340048 | tf_op jit(solution)/shard_map/reduce_scatter | solution.py:27
  239.2 5.3 convert_bitcast_fusion.2
  244.6 66.6 %reduce-scatter.14.cloned.1.call-done = bf16[128,3584]{1,0:T(8,128)(2,1)} async-done(((bf16[512,3584]{1,0:T(8,128)(2,1)}), bf16[128,3584]{1,0:T(8,128)(2,1)}) %reduce-scatter.14.cloned.1.call-update) | async-done | bytes 917520 | tf_op jit(solution)/shard_map/reduce_scatter | solution.py:30
  311.1 71.0 %reduce-scatter.10.cloned.1.call-done = bf16[128,3584]{1,0:T(8,128)(2,1)} async-done(((bf16[512,3584]{1,0:T(8,128)(2,1)}), bf16[128,3584]{1,0:T(8,128)(2,1)}) %reduce-scatter.10.cloned.1.call-update) | async-done | bytes 917520 | tf_op jit(solution)/shard_map/reduce_scatter | solution.py:30
  385.1 72.6 %all-gather.4.cloned.1.call-done = bf16[512,3584]{1,0:T(8,128)(2,1)} async-done(((bf16[128,3584]{1,0:T(8,128)(2,1)}), bf16[512,3584]{1,0:T(8,128)(2,1)}) %all-gather.4.cloned.1.call-update) | async-done | bytes 3670032 | tf_op jit(solution)/shard_map/all_gather | solution.py:39
  458.0 18.1 %all-gather.6.cloned.1.call-done = bf16[512,7168]{1,0:T(8,128)(2,1)} async-done(((bf16[512,3584]{1,0:T(8,128)(2,1)}), bf16[512,7168]{1,0:T(8,128)(2,1)}) %all-gather.6.cloned.1.call-update) | async-done | bytes 7340048 | tf_op jit(solution)/shard_map/all_gather | solution.py:40
  476.1 14.1 %fusion.41 = f32[512,1024]{1,0:T(8,128)} fusion(bf16[512,7168]{1,0:T(8,128)(2,1)} %all-gather.6.cloned.1.call-done, bf16[7168,1024]{1,0:T(8,128)(2,1)} %param.9), kind=kOutput, calls=%fused_computation.64 | convolution fusion | flops 7516192768 | bytes 24117248 | tf_op jit(solution)/shard_map/dot_general | solution.py:41
  490.3 36.5 %reduce-scatter.16.cloned.1.call-done = f32[128,1024]{1,0:T(8,128)} async-done(((f32[512,1024]{1,0:T(8,128)}), f32[128,1024]{1,0:T(8,128)}) %reduce-scatter.16.cloned.1.call-update) | async-done | bytes 524304 | tf_op jit(solution)/shard_map/reduce_scatter | solution.py:42
  528.7 26.7 %all-gather.8.cloned.1.call-done = bf16[512,1024]{1,0:T(8,128)(2,1)} async-done(((bf16[128,1024]{1,0:T(8,128)(2,1)}), bf16[512,1024]{1,0:T(8,128)(2,1)}) %all-gather.8.cloned.1.call-update) | async-done | bytes 1048592 | tf_op jit(solution)/shard_map/all_gather | solution.py:45
  555.4 14.4 %fusion.42 = f32[512,7168]{0,1:T(8,128)} fusion(bf16[512,1024]{1,0:T(8,128)(2,1)} %all-gather.8.cloned.1.call-done, bf16[7168,1024]{1,0:T(8,128)(2,1)} %param.9), kind=kOutput, calls=%fused_computation.65 | convolution fusion | flops 7516192768 | bytes 30408704 | tf_op jit(solution)/shard_map/dot_general | solution.py:49
  569.8 14.3 %copy.15 = f32[512,2,3584]{2,0,1:T(8,128)} copy(f32[512,2,3584]{0,2,1:T(8,128)} %bitcast.60) | data formatting | bytes 29360128 | tf_op jit(solution)/shard_map/reshape | solution.py:28
  584.2 24.1 %reduce-scatter.18.cloned.1.call-done = f32[512,1,3584]{2,0,1:T(8,128)} async-done(((f32[512,2,3584]{2,0,1:T(8,128)}), f32[512,1,3584]{2,0,1:T(8,128)}) %reduce-scatter.18.cloned.1.call-update) | async-done | bytes 7340048 | tf_op jit(solution)/shard_map/reduce_scatter | solution.py:27
  608.3 5.3 convert_bitcast_fusion
  620.4 62.9 %reduce-scatter.20.cloned.1.call-done = bf16[128,3584]{1,0:T(8,128)(2,1)} async-done(((bf16[512,3584]{1,0:T(8,128)(2,1)}), bf16[128,3584]{1,0:T(8,128)(2,1)}) %reduce-scatter.20.cloned.1.call-update) | async-done | bytes 917520 | tf_op jit(solution)/shard_map/reduce_scatter | solution.py:30
  683.3 3.0 fusion.15
  688.7 52.3 %all-reduce.4.cloned.1.call-done = f32[512,128]{0,1:T(8,128)} async-done(((f32[512,128]{0,1:T(8,128)}), f32[512,128]{0,1:T(8,128)}) %all-reduce.4.cloned.1.call-update) | async-done | bytes 262160 | tf_op jit(solution)/shard_map/psum | solution.py:47
  741.8 52.7 %all-reduce.6.cloned.1.call-done = f32[128,192]{0,1:T(8,128)} async-done(((f32[128,192]{0,1:T(8,128)}), f32[128,192]{0,1:T(8,128)}) %all-reduce.6.cloned.1.call-update) | async-done | bytes 98320 | tf_op jit(solution)/shard_map/psum | solution.py:62
  799.2 23.6 %all-reduce.7 = bf16[4,12288]{1,0:T(4,128)(2,1)S(1)} all-reduce(f32[4,12288]{1,0:T(4,128)} %reshape.33), channel_id=1, replica_groups=mesh['z'=4,'core'=2,'tensor'=4] {'z'}, use_global_device_ids=true, to_apply=%region_9.10 | all-reduce | flops 49152 | bytes 294912 | tf_op jit(solution)/shard_map/psum | solution.py:71
  (52 shorter events, 21.8 us)
Async XLA Ops:
  6.5 816.3 %copy-start = (bf16[128,12288]{1,0:T(8,128)(2,1)S(1)}, bf16[128,12288]{1,0:T(8,128)(2,1)}, u32[]{:S(2)}) copy-start(bf16[128,12288]{1,0:T(8,128)(2,1)} %param.13) | copy-start | bytes 9437188
  6.5 205.9 %reduce-scatter.12.cloned.1.call-start = ((), (), s32[]{:S(2)}) async-start(), calls=%async_computation.9 | async-start | bytes 22020096 | tf_op jit(solution)/shard_map/reduce_scatter | solution.py:27
  136.7 102.5 %reduce-scatter.8.cloned.1.call-start = ((), (), s32[]{:S(2)}) async-start(), calls=%async_computation.7 | async-start | bytes 22020096 | tf_op jit(solution)/shard_map/reduce_scatter | solution.py:27
  212.4 98.7 %reduce-scatter.14.cloned.1.call-start = ((), (), s32[]{:S(2)}) async-start(), calls=%async_computation.10 | async-start | bytes 4587520 | tf_op jit(solution)/shard_map/reduce_scatter | solution.py:30
  217.8 164.2 %reduce-scatter.10.cloned.1.call-start = ((), (), s32[]{:S(2)}) async-start(), calls=%async_computation.8 | async-start | bytes 4587520 | tf_op jit(solution)/shard_map/reduce_scatter | solution.py:30
  244.5 213.2 %all-gather.4.cloned.1.call-start = ((), (), s32[]{:S(2)}) async-start(), calls=%async_computation.11 | async-start | bytes 4587520 | tf_op jit(solution)/shard_map/all_gather | solution.py:39
  385.0 91.0 %all-gather.6.cloned.1.call-start = ((), (), s32[]{:S(2)}) async-start(), calls=%async_computation.12 | async-start | bytes 11010048 | tf_op jit(solution)/shard_map/all_gather | solution.py:40
  457.7 69.0 %reduce-scatter.16.cloned.1.call-start = ((), (), s32[]{:S(2)}) async-start(), calls=%async_computation.13 | async-start | bytes 2621440 | tf_op jit(solution)/shard_map/reduce_scatter | solution.py:42
  490.2 65.2 %all-gather.8.cloned.1.call-start = ((), (), s32[]{:S(2)}) async-start(), calls=%async_computation.14 | async-start | bytes 1310720 | tf_op jit(solution)/shard_map/all_gather | solution.py:45
  528.6 79.6 %reduce-scatter.18.cloned.1.call-start = ((), (), s32[]{:S(2)}) async-start(), calls=%async_computation.16 | async-start | bytes 22020096 | tf_op jit(solution)/shard_map/reduce_scatter | solution.py:27
  584.1 99.2 %reduce-scatter.20.cloned.1.call-start = ((), (), s32[]{:S(2)}) async-start(), calls=%async_computation.17 | async-start | bytes 4587520 | tf_op jit(solution)/shard_map/reduce_scatter | solution.py:30
  613.6 0.9 copy-start.1
  613.6 127.5 %all-reduce.4.cloned.1.call-start = ((), (), s32[]{:S(2)}) async-start(), calls=%async_computation.15 | async-start | bytes 524288 | tf_op jit(solution)/shard_map/psum | solution.py:47
  620.4 174.1 %all-reduce.6.cloned.1.call-start = ((), (), s32[]{:S(2)}) async-start(), calls=%async_computation.18 | async-start | bytes 196608 | tf_op jit(solution)/shard_map/psum | solution.py:62
  683.3 3.0 copy-start.2
  683.3 3.0 copy-start.3
Sparse Core Ops, SparseCore 0:
  136.8 26.6 reduce-scatter.11
  212.5 26.6 reduce-scatter.7
  241.5 69.5 reduce-scatter.13
  313.3 68.7 reduce-scatter.9
  385.2 72.4 all-gather.3
  459.1 16.9 all-gather.5
  490.3 36.3 reduce-scatter.15
  528.7 26.6 all-gather.7
  584.2 23.9 reduce-scatter.17
  613.7 69.5 reduce-scatter.19
  685.7 55.2 all-reduce.3
  744.0 50.4 all-reduce.5
where the time goes:
time: 836 us; the launch traced here: 831 us
  waiting for transfers between devices  505 us (60%)
  local copies, waits for them, and re-layouts  195 us (23%)
  matrix products  71.6 us (9%)
  blocking collectives  23.6 us (3%)
  other arithmetic  22.2 us (3%)
  between operations  13.7 us (2%)
    reduce_scatter x3, waiting for transfers between devices, over_dp(): lax.psum_scatter(part.astype(jnp.bfloat16), 'z', scatter_dimension=0, til...  200 us
    all_gather x1, waiting for transfers between devices, local(): hidden = lax.all_gather(hidden_loc, 'z', axis=0, tiled=True)  72.6 us
    dot_general x1, local copies, waits for them, and re-layouts, local(): jnp.dot(tokens, w_gate_up[:, 0, :], preferred_element_type=jnp.float32)  61.2 us
    dot_general x1, local copies, waits for them, and re-layouts, local(): jnp.dot(tokens, w_gate_up[:, 1, :], preferred_element_type=jnp.float32)  60 us
    slice x1, local copies, waits for them, and re-layouts, local(): w_gate_up[:, 0, :]  55.9 us
    psum x1, waiting for transfers between devices, local(): b_sum = lax.psum(b_part, ('core', 'tensor'))  52.7 us
    psum x1, waiting for transfers between devices, local(): lax.psum(jnp.concatenate([a_in_part, a_out_part], axis=1), ('z', 'core'))  52.3 us
    reduce_scatter x3, waiting for transfers between devices, over_dp(): lax.psum_scatter(part.reshape(total, n_core, width_h), 'core', scatter_di...  45.5 us
  transfers between devices with their start and end apart: 12, of which 11 were waited for; matrix products, arithmetic and copies ran while one was open for 12% of the time, Pallas kernels for 0%

commit v1 on v0

--- a/solution.py
+++ b/solution.py
@@ -42,7 +42,15 @@
     out_rows = lax.psum_scatter(out_part, "tensor", scatter_dimension=0, tiled=True)
     tgt_rows = lax.dynamic_slice_in_dim(targets, t_idx * rows_t, rows_t, 0)
     cot_rows = (out_rows - tgt_rows.astype(jnp.float32)).astype(jnp.bfloat16)
-    cot = lax.all_gather(cot_rows, "tensor", axis=0, tiled=True)
+    ways, here = (lax.axis_size("tensor"), lax.axis_index("tensor"))
+    grown, reach = (cot_rows, 1)
+    while reach < ways:
+        theirs = lax.ppermute(grown, "tensor", [(d, d ^ reach) for d in range(ways)])
+        mine_first = jnp.concatenate([grown, theirs], axis=0)
+        theirs_first = jnp.concatenate([theirs, grown], axis=0)
+        grown = jnp.where(here & reach == 0, mine_first, theirs_first)
+        reach = 2 * reach
+    cot = grown
     a_out_part = jnp.dot(cot, proj_model[:, RANK:], preferred_element_type=jnp.float32)
     side = lax.psum(jnp.concatenate([a_in_part, a_out_part], axis=1), ("z", "core"))
     dh = over_dp(

time: 836 us -> 834 us (level)
  waiting for transfers between devices: 505 us -> 496 us
    all_gather x1 -> x0, waiting for transfers between devices: 26.7 us -> none  [local(): cot = lax.all_gather(cot_rows, 'tensor', axis=0, tiled=True)]
    ppermute x0 -> x2, waiting for transfers between devices: none -> 18.4 us  [local(): lax.ppermute(grown, 'tensor', [(d, d ^ reach) for d in range(ways)])]
  transfers between devices with their start and end apart: 12 -> 13, of which waited for: 11 -> 12; matrix products, arithmetic and copies ran while one was open for 12% -> 12% of each run, Pallas kernels for 0% -> 0%
where the time goes in v1:
time: 834 us; the launch traced here: 829 us
  waiting for transfers between devices  496 us (59%)
  local copies, waits for them, and re-layouts  195 us (23%)
  matrix products  74.4 us (9%)
  blocking collectives  23.6 us (3%)
  other arithmetic  23.5 us (3%)
  between operations  13.4 us (2%)
    reduce_scatter x3, waiting for transfers between devices, over_dp(): lax.psum_scatter(part.astype(jnp.bfloat16), 'z', scatter_dimension=0, til...  200 us
    all_gather x1, waiting for transfers between devices, local(): hidden = lax.all_gather(hidden_loc, 'z', axis=0, tiled=True)  72.6 us
    dot_general x1, local copies, waits for them, and re-layouts, local(): jnp.dot(tokens, w_gate_up[:, 0, :], preferred_element_type=jnp.float32)  61.2 us
    dot_general x1, local copies, waits for them, and re-layouts, local(): jnp.dot(tokens, w_gate_up[:, 1, :], preferred_element_type=jnp.float32)  60 us
    slice x1, local copies, waits for them, and re-layouts, local(): w_gate_up[:, 0, :]  55.9 us
    psum x1, waiting for transfers between devices, local(): b_sum = lax.psum(b_part, ('core', 'tensor'))  52.8 us
    psum x1, waiting for transfers between devices, local(): lax.psum(jnp.concatenate([a_in_part, a_out_part], axis=1), ('z', 'core'))  52.2 us
    reduce_scatter x3, waiting for transfers between devices, over_dp(): lax.psum_scatter(part.reshape(total, n_core, width_h), 'core', scatter_di...  45.5 us
  transfers between devices with their start and end apart: 13, of which 12 were waited for; matrix products, arithmetic and copies ran while one was open for 12% of the time, Pallas kernels for 0%

profile of v1, /device:TPU:0, one launch (start us, length us, event | category | flops | bytes accessed | tf_op | source)
XLA Modules:
  0.0 829.3 jit_solution(7546818917156869686)
XLA Ops:
  6.5 55.9 %fusion.43 = (bf16[1024,1,7168]{2,1,0:T(2,128)(2,1)}, bf16[1024,1,7168]{2,1,0:T(2,128)(2,1)}) fusion(bf16[1024,2,7168]{2,1,0:T(2,128)(2,1)} %param.8), kind=kLoop, calls=%fused_computation.68 | loop fusion | bytes 58720256 | tf_op jit(solution)/shard_map/slice | solution.py:34
  62.5 60.0 %copy.21 = bf16[1024,1,7168]{0,2,1:T(8,128)(2,1)} copy(bf16[1024,1,7168]{2,1,0:T(2,128)(2,1)} %get-tuple-element.6) | data formatting | bytes 29360128 | tf_op jit(solution)/shard_map/dot_general | solution.py:35
  122.5 14.3 %fusion.9 = f32[512,2,3584]{2,0,1:T(8,128)} fusion(bf16[2,3584,1024]{2,1,0:T(8,128)(2,1)} %bitcast.56, bf16[512,1024]{1,0:T(8,128)(2,1)} %param.7), kind=kOutput, calls=%fused_computation.22 | convolution fusion | flops 7516192768 | bytes 30408704 | tf_op jit(solution)/shard_map/dot_general | solution.py:35
  136.9 61.2 %copy.20 = bf16[1024,1,7168]{0,2,1:T(8,128)(2,1)} copy(bf16[1024,1,7168]{2,1,0:T(2,128)(2,1)} %get-tuple-element.5) | data formatting | bytes 29360128 | tf_op jit(solution)/shard_map/dot_general | solution.py:34
  198.1 14.3 %fusion.11 = f32[512,2,3584]{2,0,1:T(8,128)} fusion(bf16[2,3584,1024]{2,1,0:T(8,128)(2,1)} %bitcast.57, bf16[512,1024]{1,0:T(8,128)(2,1)} %param.7), kind=kOutput, calls=%fused_computation.24 | convolution fusion | flops 7516192768 | bytes 30408704 | tf_op jit(solution)/shard_map/dot_general | solution.py:34
  212.5 5.4 convert_bitcast_fusion.1
  218.0 21.3 %reduce-scatter.8.cloned.1.call-done = f32[512,1,3584]{2,0,1:T(8,128)} async-done(((f32[512,2,3584]{2,0,1:T(8,128)}), f32[512,1,3584]{2,0,1:T(8,128)}) %reduce-scatter.8.cloned.1.call-update) | async-done | bytes 7340048 | tf_op jit(solution)/shard_map/reduce_scatter | solution.py:27
  239.3 5.3 convert_bitcast_fusion.2
  244.7 66.6 %reduce-scatter.14.cloned.1.call-done = bf16[128,3584]{1,0:T(8,128)(2,1)} async-done(((bf16[512,3584]{1,0:T(8,128)(2,1)}), bf16[128,3584]{1,0:T(8,128)(2,1)}) %reduce-scatter.14.cloned.1.call-update) | async-done | bytes 917520 | tf_op jit(solution)/shard_map/reduce_scatter | solution.py:30
  311.2 71.0 %reduce-scatter.10.cloned.1.call-done = bf16[128,3584]{1,0:T(8,128)(2,1)} async-done(((bf16[512,3584]{1,0:T(8,128)(2,1)}), bf16[128,3584]{1,0:T(8,128)(2,1)}) %reduce-scatter.10.cloned.1.call-update) | async-done | bytes 917520 | tf_op jit(solution)/shard_map/reduce_scatter | solution.py:30
  385.2 72.6 %all-gather.3.cloned.1.call-done = bf16[512,3584]{1,0:T(8,128)(2,1)} async-done(((bf16[128,3584]{1,0:T(8,128)(2,1)}), bf16[512,3584]{1,0:T(8,128)(2,1)}) %all-gather.3.cloned.1.call-update) | async-done | bytes 3670032 | tf_op jit(solution)/shard_map/all_gather | solution.py:39
  458.0 18.1 %all-gather.5.cloned.1.call-done = bf16[512,7168]{1,0:T(8,128)(2,1)} async-done(((bf16[512,3584]{1,0:T(8,128)(2,1)}), bf16[512,7168]{1,0:T(8,128)(2,1)}) %all-gather.5.cloned.1.call-update) | async-done | bytes 7340048 | tf_op jit(solution)/shard_map/all_gather | solution.py:40
  476.1 14.1 %fusion.44 = f32[512,1024]{1,0:T(8,128)} fusion(bf16[512,7168]{1,0:T(8,128)(2,1)} %all-gather.5.cloned.1.call-done, bf16[7168,1024]{1,0:T(8,128)(2,1)} %param.9), kind=kOutput, calls=%fused_computation.69 | convolution fusion | flops 7516192768 | bytes 24117248 | tf_op jit(solution)/shard_map/dot_general | solution.py:41
  490.3 36.5 %reduce-scatter.16.cloned.1.call-done = f32[128,1024]{1,0:T(8,128)} async-done(((f32[512,1024]{1,0:T(8,128)}), f32[128,1024]{1,0:T(8,128)}) %reduce-scatter.16.cloned.1.call-update) | async-done | bytes 524304 | tf_op jit(solution)/shard_map/reduce_scatter | solution.py:42
  529.5 6.7 collective-permute-done
  539.7 11.7 %collective-permute-done.1 = bf16[256,1024]{1,0:T(8,128)(2,1)} collective-permute-done((bf16[256,1024]{1,0:T(8,128)(2,1)}, bf16[256,1024]{1,0:T(8,128)(2,1)}, u32[]{:S(2)}, u32[]{:S(2)}) %collective-permute-start.1) | collective-permute-done | bytes 524320 | tf_op jit(solution)/shard_map/ppermute | solution.py:48
  551.3 16.8 %fusion.27 = f32[512,7168]{0,1:T(8,128)} fusion(bf16[7168,1024]{1,0:T(8,128)(2,1)} %param.9, bf16[256,1024]{1,0:T(8,128)(2,1)} %collective-permute-done.1, bf16[256,1024]{1,0:T(8,128)(2,1)} %maximum_select_fusion.1, pred[]{:T(512)S(6)} %eq.19), kind=kOutput, calls=%fused_computation.42 | convolution fusion | flops 7520911360 | bytes 30408704 | tf_op jit(solution)/shard_map/dot_general | solution.py:57
  568.1 14.3 %copy.15 = f32[512,2,3584]{2,0,1:T(8,128)} copy(f32[512,2,3584]{0,2,1:T(8,128)} %bitcast.58) | data formatting | bytes 29360128 | tf_op jit(solution)/shard_map/reshape | solution.py:28
  582.5 24.1 %reduce-scatter.18.cloned.1.call-done = f32[512,1,3584]{2,0,1:T(8,128)} async-done(((f32[512,2,3584]{2,0,1:T(8,128)}), f32[512,1,3584]{2,0,1:T(8,128)}) %reduce-scatter.18.cloned.1.call-update) | async-done | bytes 7340048 | tf_op jit(solution)/shard_map/reduce_scatter | solution.py:27
  606.7 5.3 convert_bitcast_fusion
  619.2 62.5 %reduce-scatter.20.cloned.1.call-done = bf16[128,3584]{1,0:T(8,128)(2,1)} async-done(((bf16[512,3584]{1,0:T(8,128)(2,1)}), bf16[128,3584]{1,0:T(8,128)(2,1)}) %reduce-scatter.20.cloned.1.call-update) | async-done | bytes 917520 | tf_op jit(solution)/shard_map/reduce_scatter | solution.py:30
  687.1 52.2 %all-reduce.4.cloned.1.call-done = f32[512,128]{0,1:T(8,128)} async-done(((f32[512,128]{0,1:T(8,128)}), f32[512,128]{0,1:T(8,128)}) %all-reduce.4.cloned.1.call-update) | async-done | bytes 262160 | tf_op jit(solution)/shard_map/psum | solution.py:55
  740.1 52.8 %all-reduce.6.cloned.1.call-done = f32[128,192]{0,1:T(8,128)} async-done(((f32[128,192]{0,1:T(8,128)}), f32[128,192]{0,1:T(8,128)}) %all-reduce.6.cloned.1.call-update) | async-done | bytes 98320 | tf_op jit(solution)/shard_map/psum | solution.py:70
  797.7 23.6 %all-reduce.7 = bf16[4,12288]{1,0:T(4,128)(2,1)S(1)} all-reduce(f32[4,12288]{1,0:T(4,128)} %reshape.33), channel_id=1, replica_groups=mesh['z'=4,'core'=2,'tensor'=4] {'z'}, use_global_device_ids=true, to_apply=%region_9.10 | all-reduce | flops 49152 | bytes 294912 | tf_op jit(solution)/shard_map/psum | solution.py:79
  (54 shorter events, 29.3 us)
Async XLA Ops:
  6.5 814.7 %copy-start = (bf16[128,12288]{1,0:T(8,128)(2,1)S(1)}, bf16[128,12288]{1,0:T(8,128)(2,1)}, u32[]{:S(2)}) copy-start(bf16[128,12288]{1,0:T(8,128)(2,1)} %param.13) | copy-start | bytes 9437188
  6.5 206.0 %reduce-scatter.12.cloned.1.call-start = ((), (), s32[]{:S(2)}) async-start(), calls=%async_computation.9 | async-start | bytes 22020096 | tf_op jit(solution)/shard_map/reduce_scatter | solution.py:27
  136.8 102.5 %reduce-scatter.8.cloned.1.call-start = ((), (), s32[]{:S(2)}) async-start(), calls=%async_computation.7 | async-start | bytes 22020096 | tf_op jit(solution)/shard_map/reduce_scatter | solution.py:27
  212.4 98.8 %reduce-scatter.14.cloned.1.call-start = ((), (), s32[]{:S(2)}) async-start(), calls=%async_computation.10 | async-start | bytes 4587520 | tf_op jit(solution)/shard_map/reduce_scatter | solution.py:30
  217.9 164.3 %reduce-scatter.10.cloned.1.call-start = ((), (), s32[]{:S(2)}) async-start(), calls=%async_computation.8 | async-start | bytes 4587520 | tf_op jit(solution)/shard_map/reduce_scatter | solution.py:30
  244.6 213.2 %all-gather.3.cloned.1.call-start = ((), (), s32[]{:S(2)}) async-start(), calls=%async_computation.11 | async-start | bytes 4587520 | tf_op jit(solution)/shard_map/all_gather | solution.py:39
  385.1 91.0 %all-gather.5.cloned.1.call-start = ((), (), s32[]{:S(2)}) async-start(), calls=%async_computation.12 | async-start | bytes 11010048 | tf_op jit(solution)/shard_map/all_gather | solution.py:40
  457.8 69.0 %reduce-scatter.16.cloned.1.call-start = ((), (), s32[]{:S(2)}) async-start(), calls=%async_computation.13 | async-start | bytes 2621440 | tf_op jit(solution)/shard_map/reduce_scatter | solution.py:42
  490.3 116.4 %reduce-scatter.18.cloned.1.call-start = ((), (), s32[]{:S(2)}) async-start(), calls=%async_computation.15 | async-start | bytes 22020096 | tf_op jit(solution)/shard_map/reduce_scatter | solution.py:27
  528.0 8.2 collective-permute-start
  538.2 13.1 %collective-permute-start.1 = (bf16[256,1024]{1,0:T(8,128)(2,1)}, bf16[256,1024]{1,0:T(8,128)(2,1)}, u32[]{:S(2)}, u32[]{:S(2)}) collective-permute-start(bf16[256,1024]{1,0:T(8,128)(2,1)} %maximum_select_fusion.1), channel_id=1, source_target_pairs={{0,2},{1,3},{2,0},{3,1},{4,6},{5,7},{6,4},{7,5},{8,10},{9,11},{10,... | collective-permute-start | bytes 1572872 | tf_op jit(solution)/shard_map/ppermute | solution.py:48
  582.5 99.2 %reduce-scatter.20.cloned.1.call-start = ((), (), s32[]{:S(2)}) async-start(), calls=%async_computation.16 | async-start | bytes 4587520 | tf_op jit(solution)/shard_map/reduce_scatter | solution.py:30
  611.9 0.9 copy-start.2
  612.0 127.4 %all-reduce.4.cloned.1.call-start = ((), (), s32[]{:S(2)}) async-start(), calls=%async_computation.14 | async-start | bytes 524288 | tf_op jit(solution)/shard_map/psum | solution.py:55
  619.1 173.8 %all-reduce.6.cloned.1.call-start = ((), (), s32[]{:S(2)}) async-start(), calls=%async_computation.17 | async-start | bytes 196608 | tf_op jit(solution)/shard_map/psum | solution.py:70
  681.7 3.0 copy-start.1
  681.7 3.0 copy-start.3
Sparse Core Ops, SparseCore 0:
  137.0 26.6 reduce-scatter.11
  212.6 26.6 reduce-scatter.7
  241.6 69.5 reduce-scatter.13
  313.4 68.7 reduce-scatter.9
  385.2 72.4 all-gather.2
  459.2 16.9 all-gather.4
  490.4 36.3 reduce-scatter.15
  582.6 23.9 reduce-scatter.17
  612.1 69.5 reduce-scatter.19
  684.0 55.3 all-reduce.3
  742.4 50.4 all-reduce.5
